TPU v7x, 128 devices: a whole 4x4x4 slice. The times are simulated.
128 devices in a mesh: dom: 16 (over z, y), grp: 8 (over x, core).
Axes of the slice: x: 4, y: 4, z: 4, core: 2. Of those that a mesh axis runs over, the one named last changes fastest.
Arguments:
- residual_in: bfloat16 [1024, 32, 625], P(('dom', 'grp')), may hold values from -6 to 6
- block_inverse: bfloat16 [1024, 625, 625], P(('dom', 'grp')), may hold values from -0.25 to 0.25
- coupling: bfloat16 [2048, 625, 625], P(('dom', 'grp')), may hold values from -0.25 to 0.25
- tile_region: int32 [2048, 1], P(('dom', 'grp')), may hold values from 0 to 15; in each aligned block of 16 rows (0 to 15, 16 to 31, ...) at most 2 rows name the same one
- tile_source: int32 [2048], P(('dom', 'grp')), may hold values from 0 to 7
- tile_target: int32 [2048], P(('dom', 'grp')), may hold values from 0 to 7
- interface_basis: bfloat16 [1024, 625, 64], P(('dom', 'grp')), may hold values from -0.25 to 0.25
- reduced_inverse: float32 [16, 64, 64], P('dom'), may hold values from -0.75 to 0.75
Outputs:
- preconditioned: float32 [1024, 32, 625], P(('dom', 'grp'))
Inputs may be any that keep to these rules, and one draw needn't show every extreme that they name: `tile_region`: among the 16 tiles of one device, at most 2 name the same region; in every draw some device names some region exactly 2 times.
All inputs are finite; a program needn't handle non-finite values.
Results may differ from a plain program's by a relative error of at most 0.013.
Values may be sent and summed in bfloat16 or wider, within the bound.
No kernel may reach another device: no remote copies, remote signals or barrier semaphores. Data moves between devices by JAX's collectives and lax.ppermute only.
A program may use at most 256 MiB of HBM per device.

v0:
```python
import jax
import jax.numpy as jnp
from jax import lax
from jax.sharding import PartitionSpec as P

CAP = 2
LANE = 128


def group_sum(value, axis):
    size = lax.axis_size(axis)
    if size & size - 1:
        return lax.psum(value, axis)
    bit = 1
    while bit < size:
        pairs = [(i, i ^ bit) for i in range(size)]
        value = value + lax.ppermute(value, axis, pairs)
        bit *= 2
    return value


def shards(
    residual_in,
    block_inverse,
    coupling,
    tile_region,
    tile_source,
    tile_target,
    interface_basis,
    reduced_inverse,
):
    regions = lax.axis_size("dom")
    slots = regions * CAP
    elements = residual_in.shape[0]
    vectors = residual_in.shape[1]
    width = residual_in.shape[2]
    tiles = coupling.shape[0]
    padded = -(-(width + 1) // LANE) * LANE
    initial = jnp.einsum(
        "ekb,ebc->ekc", residual_in, block_inverse, preferred_element_type=jnp.float32
    ).astype(jnp.bfloat16)
    info = lax.optimization_barrier(jnp.concatenate([tile_region[:, 0], tile_source, tile_target]))
    destination = info[:tiles]
    tile_source = info[tiles : 2 * tiles]
    tile_target = info[2 * tiles :]
    order = jnp.arange(tiles, dtype=jnp.int32)
    same = destination[:, None] == destination[None, :]
    tile_rank = jnp.sum(same & (order[None, :] < order[:, None]), axis=1).astype(jnp.int32)
    slot_index = destination * CAP + tile_rank
    slot_ids = jnp.arange(slots, dtype=jnp.int32)
    hit = slot_index[None, :] == slot_ids[:, None]
    slot_tile = jnp.where(
        jnp.any(hit, axis=1), jnp.sum(jnp.where(hit, order[None, :], 0), axis=1), tiles
    ).astype(jnp.int32)
    sources = initial[tile_source]
    middle = tiles // 2
    local_products = jnp.concatenate(
        [
            jnp.einsum(
                "tkb,tbc->tkc",
                sources[:middle],
                coupling[:middle],
                preferred_element_type=jnp.float32,
            ),
            jnp.einsum(
                "tkb,tbc->tkc",
                sources[middle:],
                coupling[middle:],
                preferred_element_type=jnp.float32,
            ),
        ],
        axis=0,
    ).astype(jnp.bfloat16)
    marks = jnp.concatenate([tile_target, jnp.full((1,), -1, jnp.int32)]).astype(jnp.bfloat16)
    column = lax.broadcasted_iota(jnp.int32, (tiles + 1, vectors, padded - width), 2)
    row = lax.broadcasted_iota(jnp.int32, (tiles + 1, vectors, padded - width), 1)
    tail = jnp.where((column == 0) & (row == 0), marks[:, None, None], jnp.bfloat16(0))
    body = jnp.concatenate([local_products, jnp.zeros((1, vectors, width), jnp.bfloat16)], axis=0)
    extended = jnp.concatenate([body, tail], axis=2)
    product_buffer = extended[slot_tile]
    received = lax.all_to_all(
        product_buffer.reshape(regions, CAP, vectors, padded),
        "dom",
        split_axis=0,
        concat_axis=0,
        tiled=True,
    ).reshape(slots, vectors, padded)
    targets = received[:, 0, width].astype(jnp.int32)
    products = received[:, :, :width]
    selector = (targets[None, :] == jnp.arange(elements, dtype=jnp.int32)[:, None]).astype(
        jnp.bfloat16
    )
    coupled = jnp.einsum("es,skc->ekc", selector, products, preferred_element_type=jnp.float32)
    corrected_in = (residual_in.astype(jnp.float32) - coupled).astype(jnp.bfloat16)
    projected = jnp.einsum(
        "ebc,ecm->ebm", block_inverse, interface_basis, preferred_element_type=jnp.float32
    )
    partial_reduced = jnp.einsum(
        "ekb,ebm->km",
        corrected_in,
        lax.optimization_barrier(projected.astype(jnp.bfloat16)),
        preferred_element_type=jnp.float32,
    )
    reduced = group_sum(partial_reduced, "grp")
    half = elements // 2
    second = jnp.concatenate(
        [
            jnp.einsum(
                "ekb,ebc->ekc",
                corrected_in[:half],
                block_inverse[:half],
                preferred_element_type=jnp.float32,
            ),
            jnp.einsum(
                "ekb,ebc->ekc",
                corrected_in[half:],
                block_inverse[half:],
                preferred_element_type=jnp.float32,
            ),
        ],
        axis=0,
    )
    solved = jnp.dot(
        reduced,
        reduced_inverse[0],
        precision=lax.Precision.HIGHEST,
        preferred_element_type=jnp.float32,
    ).astype(jnp.bfloat16)
    correction = jnp.einsum(
        "km,ebm->ekb", solved, interface_basis, preferred_element_type=jnp.float32
    )
    return second + correction


def solution(mesh):
    return jax.shard_map(
        shards,
        mesh=mesh,
        in_specs=(
            P(("dom", "grp"), None, None),
            P(("dom", "grp"), None, None),
            P(("dom", "grp"), None, None),
            P(("dom", "grp"), None),
            P(("dom", "grp")),
            P(("dom", "grp")),
            P(("dom", "grp"), None, None),
            P("dom", None, None),
        ),
        out_specs=P(("dom", "grp"), None, None),
        check_vma=False,
    )
```

profile of v0, /device:TPU:0, one launch (start us, length us, event | category | flops | bytes accessed | tf_op | source)
XLA Modules:
  0.0 69.1 jit_solution(7914102216442023581)
XLA Ops:
  0.0 0.0 copy-start
  0.0 0.8 %pad_add_fusion = s32[48]{0:T(128)S(1)} fusion(s32[16]{0:T(128)} %param.13, s32[16]{0:T(128)} %param.12, s32[16]{0:T(128)} %bitcast.36), kind=kLoop, calls=%fused_computation.49 | loop fusion | flops 96 | bytes 384 | tf_op jit(solution)/shard_map/concatenate | solution.py:42
  0.8 0.2 convert_reduce_fusion.1
  1.0 0.1 multiply_add_fusion
  1.1 0.1 fusion.32
  1.2 0.1 select_reduce_fusion
  1.3 0.0 copy-start.2
  1.3 0.0 copy-start.4
  1.3 11.4 %fusion.40 = (bf16[8,625,625]{2,0,1:T(8,128)(2,1)}, bf16[8,625,625]{2,0,1:T(8,128)(2,1)}) fusion(bf16[16,625,625]{2,0,1:T(8,128)(2,1)} %param.10), kind=kLoop, calls=%fused_computation.56 | loop fusion | bytes 25000000 | tf_op jit(solution)/shard_map/slice | solution.py:62
  12.7 0.0 copy-done.2
  12.7 0.0 copy-done.4
  12.7 2.3 %convolution_convert_fusion.1 = bf16[8,32,625]{2,1,0:T(8,128)(2,1)S(1)} fusion(bf16[8,32,625]{2,1,0:T(8,128)(2,1)S(1)} %copy-done.4, bf16[8,625,625]{2,0,1:T(8,128)(2,1)S(1)} %copy-done.2), kind=kOutput, calls=%fused_computation.22 | convolution fusion | flops 200160000 | bytes 6890000 | tf_op jit(solution)/shard_map/ekb,ebc->ekc/dot_general | solution.py:39
  15.0 0.0 slice-start.2
  15.0 1.5 %gather_fusion = bf16[16,32,625]{2,1,0:T(8,128)(2,1)} fusion(bf16[8,32,625]{2,1,0:T(8,128)(2,1)S(1)} %convolution_convert_fusion.1, s32[1024]{0:T(1024)S(1)} %pad_clamp_fusion.1), kind=kCustom, calls=%fused_computation | custom fusion | bytes 1280064 | tf_op jit(solution)/shard_map/gather | solution.py:55
  16.4 0.0 slice-start.3
  16.4 0.0 copy-start.3
  16.4 4.3 %fusion.19 = bf16[8,32,625]{2,1,0:T(8,128)(2,1)S(1)} fusion(bf16[16,32,625]{2,1,0:T(8,128)(2,1)} %gather_fusion, bf16[8,625,625]{2,0,1:T(8,128)(2,1)} %get-tuple-element.5), kind=kOutput, calls=%fused_computation.20 | convolution fusion | flops 200160000 | bytes 7210000 | tf_op jit(solution)/shard_map/tkb,tbc->tkc/dot_general | solution.py:59
  20.7 0.0 slice-done.2
  20.7 0.1 slice-done.3
  20.8 0.0 copy-done.3
  20.8 1.2 %fusion.22 = bf16[8,32,625]{2,1,0:T(8,128)(2,1)S(1)} fusion(bf16[16,32,625]{2,1,0:T(8,128)(2,1)S(1)} %copy-done.3, bf16[8,625,625]{2,0,1:T(8,128)(2,1)S(1)} %bitcast.33), kind=kOutput, calls=%fused_computation.21 | convolution fusion | flops 200160000 | bytes 7210000 | tf_op jit(solution)/shard_map/tkb,tbc->tkc/dot_general | solution.py:65
  22.0 0.1 slice.45
  22.1 0.1 fusion.26
  22.1 0.1 pad_maximum_fusion.1
  22.2 0.1 and_select_fusion
  22.3 0.1 pad_maximum_fusion
  22.4 1.9 %gather_fusion.1 = bf16[32,32,640]{2,1,0:T(8,128)(2,1)} fusion(bf16[17,32,640]{2,1,0:T(8,128)(2,1)S(1)} %pad_maximum_fusion, s32[1024]{0:T(1024)S(1)} %pad_clamp_fusion), kind=kCustom, calls=%fused_computation.1 | custom fusion | bytes 2621568 | tf_op jit(solution)/shard_map/gather | solution.py:80
  24.3 0.0 slice-start
  24.3 8.3 %all-to-all-start = ((bf16[16,2,32,640]{3,2,1,0:T(8,128)(2,1)}), bf16[16,2,32,640]{3,2,1,0:T(8,128)(2,1)}, u32[]{:S(2)}, u32[]{:S(2)}) async-start(bf16[16,2,32,640]{3,2,1,0:T(8,128)(2,1)} %bitcast.34), calls=%async_computation | async-start | bytes 2621440 | tf_op jit(solution)/shard_map/all_to_all | solution.py:81
  32.6 0.0 slice-start.1
  32.7 6.5 %copy.30 = bf16[8,625,625]{2,1,0:T(8,128)(2,1)} copy(bf16[8,625,625]{2,0,1:T(8,128)(2,1)} %param.9) | data formatting | bytes 12500000 | tf_op args[1]
  39.2 0.0 copy-done
  39.2 0.0 slice-done
  39.2 0.0 slice-done.1
  39.2 2.2 %convolution_convert_fusion = bf16[8,625,64]{1,2,0:T(8,128)(2,1)S(1)} fusion(bf16[8,625,64]{1,2,0:T(8,128)(2,1)S(1)} %copy-done, bf16[8,625,625]{2,0,1:T(8,128)(2,1)S(1)} %bitcast.31), kind=kOutput, calls=%fused_computation.13 | convolution fusion | flops 400320000 | bytes 7530000 | tf_op jit(solution)/shard_map/ebc,ecm->ebm/dot_general | solution.py:95
  41.4 0.0 copy-start.5
  41.4 12.2 %all-to-all-done = bf16[16,2,32,640]{3,2,1,0:T(8,128)(2,1)} async-done(((bf16[16,2,32,640]{3,2,1,0:T(8,128)(2,1)}), bf16[16,2,32,640]{3,2,1,0:T(8,128)(2,1)}, u32[]{:S(2)}, u32[]{:S(2)}) %all-to-all-start) | async-done | bytes 1310752 | tf_op jit(solution)/shard_map/all_to_all | solution.py:81
  53.6 0.0 copy-start.1
  53.6 1.1 %slice.57 = bf16[32,1,1]{2,1,0:T(2,128)(2,1)S(1)} slice(bf16[32,32,640]{2,1,0:T(8,128)(2,1)} %bitcast.4), slice={[0:32], [0:1], [625:626]} | slice | bytes 128 | tf_op jit(solution)/shard_map/slice | solution.py:88
  54.7 0.1 convert_reduce_fusion
  54.8 2.2 %fusion.16 = bf16[8,32,625]{2,0,1:T(8,128)(2,1)S(1)} fusion(bf16[32,32,625]{2,1,0:T(8,128)(2,1)} %bitcast.29, bf16[8,32,625]{2,1,0:T(8,128)(2,1)} %param.8, s32[32]{0:T(128)S(1)} %convert_reduce_fusion), kind=kOutput, calls=%fused_computation.19 | convolution fusion | flops 10720256 | bytes 1920128 | tf_op jit(solution)/shard_map/es,skc->ekc/dot_general | solution.py:93
  57.0 0.3 convolution_bitcast_fusion.1
  57.3 0.0 collective-permute-start
  57.3 0.1 fusion.41
  57.4 1.1 %collective-permute-done = f32[32,64]{1,0:T(8,128)S(1)} collective-permute-done((f32[32,64]{1,0:T(8,128)S(1)}, f32[32,64]{1,0:T(8,128)S(1)}, u32[]{:S(2)}, u32[]{:S(2)}) %collective-permute-start) | collective-permute-done | bytes 8224 | tf_op jit(solution)/shard_map/ppermute | solution.py:17
  58.5 1.5 %collective-permute-start.1 = (f32[32,64]{1,0:T(8,128)S(1)}, f32[32,64]{1,0:T(8,128)S(1)}, u32[]{:S(2)}, u32[]{:S(2)}) collective-permute-start(f32[32,64]{1,0:T(8,128)S(1)} %add.37), channel_id=1, source_target_pairs={{0,2},{1,3},{2,0},{3,1},{4,6},{5,7},{6,4},{7,5},{8,10},{9,11},{10,... | collective-permute-start | bytes 24584 | tf_op jit(solution)/shard_map/ppermute | solution.py:17
  60.0 2.5 %fusion.4 = f32[4,32,625]{2,1,0:T(8,128)S(1)} fusion(bf16[8,625,625]{2,1,0:T(8,128)(2,1)} %copy.30, bf16[4,32,625]{2,0,1:T(4,128)(2,1)S(1)} %get-tuple-element.8), kind=kOutput, calls=%fused_computation.6 | convolution fusion | flops 100000000 | bytes 3715840 | tf_op jit(solution)/shard_map/ekb,ebc->ekc/dot_general | solution.py:114
  62.5 0.0 collective-permute-done.1
  62.5 2.8 %collective-permute-start.2 = (f32[32,64]{1,0:T(8,128)S(1)}, f32[32,64]{1,0:T(8,128)S(1)}, u32[]{:S(2)}, u32[]{:S(2)}) collective-permute-start(f32[32,64]{1,0:T(8,128)S(1)} %add.38), channel_id=1, source_target_pairs={{0,4},{1,5},{2,6},{3,7},{4,0},{5,1},{6,2},{7,3},{8,12},{9,13},{10,... | collective-permute-start | bytes 24584 | tf_op jit(solution)/shard_map/ppermute | solution.py:17
  65.3 0.0 copy-done.1
  65.3 0.6 fusion.6
  66.0 1.9 %collective-permute-done.2 = f32[32,64]{1,0:T(8,128)S(1)} collective-permute-done((f32[32,64]{1,0:T(8,128)S(1)}, f32[32,64]{1,0:T(8,128)S(1)}, u32[]{:S(2)}, u32[]{:S(2)}) %collective-permute-start.2) | collective-permute-done | bytes 8224 | tf_op jit(solution)/shard_map/ppermute | solution.py:17
  67.8 0.0 copy-done.5
  67.8 0.1 fusion.25
  68.0 1.1 %fusion.15 = f32[8,32,625]{2,1,0:T(8,128)} fusion(bf16[32,64,1]{1,0,2:T(8,128)(2,1)S(1)} %fusion.25, bf16[8,625,64]{1,2,0:T(8,128)(2,1)S(1)} %copy-done, f32[4,32,625]{2,1,0:T(8,128)S(1)} %fusion.4, f32[4,32,625]{2,1,0:T(8,128)S(1)} %fusion.6), kind=kOutput, calls=%fused_computation.18 | convolution fusion | flops 20800000 | bytes 1924096 | tf_op jit(solution)/shard_map/km,ebm->ekb/dot_general | solution.py:129
  (10 shorter events, 0.0 us)
Async XLA Ops:
  0.0 39.2 %copy-start = (bf16[8,625,64]{1,2,0:T(8,128)(2,1)S(1)}, bf16[8,625,64]{1,2,0:T(8,128)(2,1)}, u32[]{:S(2)}) copy-start(bf16[8,625,64]{1,2,0:T(8,128)(2,1)} %param.14) | copy-start | bytes 1920004
  1.3 11.4 %copy-start.2 = (bf16[8,625,625]{2,0,1:T(8,128)(2,1)S(1)}, bf16[8,625,625]{2,0,1:T(8,128)(2,1)}, u32[]{:S(2)}) copy-start(bf16[8,625,625]{2,0,1:T(8,128)(2,1)} %param.9) | copy-start | bytes 18750004
  1.3 11.4 %copy-start.4 = (bf16[8,32,625]{2,1,0:T(8,128)(2,1)S(1)}, bf16[8,32,625]{2,1,0:T(8,128)(2,1)}, u32[]{:S(2)}) copy-start(bf16[8,32,625]{2,1,0:T(8,128)(2,1)} %param.8) | copy-start | bytes 960004
  15.0 5.7 %slice-start.2 = ((s8[6400000]{0:T(1024)(128)(4,1)}), s8[2205696]{0:T(1024)(128)(4,1)S(1)}, s32[]{:S(2)}) async-start(s8[6400000]{0:T(1024)(128)(4,1)} %bitcast.32), calls=%async_computation.3 | async-start | bytes 4411392
  16.4 4.4 %slice-start.3 = ((s8[6400000]{0:T(1024)(128)(4,1)}), s8[4194304]{0:T(1024)(128)(4,1)S(1)}, s32[]{:S(2)}) async-start(s8[6400000]{0:T(1024)(128)(4,1)} %bitcast.32), calls=%async_computation.4 | async-start | bytes 8388608
  16.4 4.4 %copy-start.3 = (bf16[16,32,625]{2,1,0:T(8,128)(2,1)S(1)}, bf16[16,32,625]{2,1,0:T(8,128)(2,1)}, u32[]{:S(2)}) copy-start(bf16[16,32,625]{2,1,0:T(8,128)(2,1)} %gather_fusion) | copy-start | bytes 1920004
  24.3 14.9 %slice-start = ((s8[6400000]{0:T(1024)(128)(4,1)}), s8[2205696]{0:T(1024)(128)(4,1)S(1)}, s32[]{:S(2)}) async-start(s8[6400000]{0:T(1024)(128)(4,1)} %bitcast.30), calls=%async_computation.1 | async-start | bytes 4411392
  24.3 29.3 %all-to-all-start = ((bf16[16,2,32,640]{3,2,1,0:T(8,128)(2,1)}), bf16[16,2,32,640]{3,2,1,0:T(8,128)(2,1)}, u32[]{:S(2)}, u32[]{:S(2)}) async-start(bf16[16,2,32,640]{3,2,1,0:T(8,128)(2,1)} %bitcast.34), calls=%async_computation | async-start | bytes 2621440 | tf_op jit(solution)/shard_map/all_to_all | solution.py:81
  32.6 6.5 %slice-start.1 = ((s8[6400000]{0:T(1024)(128)(4,1)}), s8[4194304]{0:T(1024)(128)(4,1)S(1)}, s32[]{:S(2)}) async-start(s8[6400000]{0:T(1024)(128)(4,1)} %bitcast.30), calls=%async_computation.2 | async-start | bytes 8388608
  41.4 26.4 %copy-start.5 = (f32[1,64,64]{2,1,0:T(8,128)S(1)}, f32[1,64,64]{2,1,0:T(8,128)}, u32[]{:S(2)}) copy-start(f32[1,64,64]{2,1,0:T(8,128)} %param.15) | copy-start | bytes 49156
  53.6 11.7 %copy-start.1 = (bf16[8,625,625]{2,1,0:T(8,128)(2,1)S(1)}, bf16[8,625,625]{2,1,0:T(8,128)(2,1)}, u32[]{:S(2)}) copy-start(bf16[8,625,625]{2,1,0:T(8,128)(2,1)} %copy.30) | copy-start | bytes 18750004
  57.3 1.2 %collective-permute-start = (f32[32,64]{1,0:T(8,128)S(1)}, f32[32,64]{1,0:T(8,128)S(1)}, u32[]{:S(2)}, u32[]{:S(2)}) collective-permute-start(f32[32,64]{1,0:T(8,128)S(1)} %convolution_bitcast_fusion.1), channel_id=1, source_target_pairs={{0,1},{1,0},{2,3},{3,2},{4,5},{5,4},{6,7},{7,6},{8,9},{9,8},{10,11... | collective-permute-start | bytes 24584 | tf_op jit(solution)/shard_map/ppermute | solution.py:17
  58.5 4.0 %collective-permute-start.1 = (f32[32,64]{1,0:T(8,128)S(1)}, f32[32,64]{1,0:T(8,128)S(1)}, u32[]{:S(2)}, u32[]{:S(2)}) collective-permute-start(f32[32,64]{1,0:T(8,128)S(1)} %add.37), channel_id=1, source_target_pairs={{0,2},{1,3},{2,0},{3,1},{4,6},{5,7},{6,4},{7,5},{8,10},{9,11},{10,... | collective-permute-start | bytes 24584 | tf_op jit(solution)/shard_map/ppermute | solution.py:17
  62.5 5.3 %collective-permute-start.2 = (f32[32,64]{1,0:T(8,128)S(1)}, f32[32,64]{1,0:T(8,128)S(1)}, u32[]{:S(2)}, u32[]{:S(2)}) collective-permute-start(f32[32,64]{1,0:T(8,128)S(1)} %add.38), channel_id=1, source_target_pairs={{0,4},{1,5},{2,6},{3,7},{4,0},{5,1},{6,2},{7,3},{8,12},{9,13},{10,... | collective-permute-start | bytes 24584 | tf_op jit(solution)/shard_map/ppermute | solution.py:17
where the time goes:
time: 69.3 us; the launch traced here: 69.1 us
  local copies, waits for them, and re-layouts  22.6 us (33%)
  matrix products  16.7 us (24%)
  waiting for transfers between devices  15.2 us (22%)
  starting transfers between devices  12.7 us (18%)
  other arithmetic  1.77 us (3%)
    all_to_all x1, waiting for transfers between devices, shards(): lax.all_to_all(product_buffer.reshape(regions, CAP, vectors, padded), 'do...  12.2 us
    slice x1, local copies, waits for them, and re-layouts, shards(): coupling[:middle]  11.4 us
    all_to_all x1, starting transfers between devices, shards(): lax.all_to_all(product_buffer.reshape(regions, CAP, vectors, padded), 'do...  8.34 us
    unnamed x21, local copies, waits for them, and re-layouts  6.64 us
    ppermute x3, starting transfers between devices, group_sum(): value = value + lax.ppermute(value, axis, pairs)  4.31 us
    dot_general x1, matrix products, shards(): jnp.einsum('tkb,tbc->tkc', sources[:middle], coupling[:middle], preferred...  4.25 us
    ppermute x3, waiting for transfers between devices, group_sum(): value = value + lax.ppermute(value, axis, pairs)  2.94 us
    dot_general x1, matrix products, shards(): jnp.einsum('ekb,ebc->ekc', corrected_in[half:], block_inverse[half:], pre...  2.53 us
  transfers between devices with their start and end apart: 4, of which 3 were waited for; matrix products, arithmetic and copies ran while one was open for 17% of the time, Pallas kernels for 0%

commit v1 on v0

--- a/solution.py
+++ b/solution.py
@@ -5,6 +5,22 @@
 
 CAP = 2
 LANE = 128
+
+
+def swapped_with_each(value, axis, split, join):
+    ways, here = (lax.axis_size(axis), lax.axis_index(axis))
+    width = value.shape[split] // ways
+    shape = list(value.shape)
+    shape[split] = width
+    height = shape[join]
+    shape[join] = height * ways
+    full = jnp.zeros(shape, value.dtype)
+    for mask in range(ways):
+        part = lax.dynamic_slice_in_dim(value, (here ^ mask) * width, width, axis=split)
+        if mask:
+            part = lax.ppermute(part, axis, [(d, d ^ mask) for d in range(ways)])
+        full = lax.dynamic_update_slice_in_dim(full, part, (here ^ mask) * height, axis=join)
+    return full
 
 
 def group_sum(value, axis):
@@ -78,12 +94,8 @@
     body = jnp.concatenate([local_products, jnp.zeros((1, vectors, width), jnp.bfloat16)], axis=0)
     extended = jnp.concatenate([body, tail], axis=2)
     product_buffer = extended[slot_tile]
-    received = lax.all_to_all(
-        product_buffer.reshape(regions, CAP, vectors, padded),
-        "dom",
-        split_axis=0,
-        concat_axis=0,
-        tiled=True,
+    received = swapped_with_each(
+        product_buffer.reshape(regions, CAP, vectors, padded), "dom", 0, 0
     ).reshape(slots, vectors, padded)
     targets = received[:, 0, width].astype(jnp.int32)
     products = received[:, :, :width]

time: 69.3 us -> 90.4 us (1.30)
  starting transfers between devices: 12.7 us -> 37.6 us
  waiting for transfers between devices: 15.2 us -> 10.3 us
  matrix products: 16.7 us -> 19.8 us
  local copies, waits for them, and re-layouts: 22.6 us -> 20.1 us
    ppermute x0 -> x15, starting transfers between devices: none -> 33.3 us  [swapped_with_each(): part = lax.ppermute(part, axis, [(d, d ^ mask) for d in range(ways)])]
    all_to_all x1 -> x0, waiting for transfers between devices: 12.2 us -> none  [shards(): lax.all_to_all(product_buffer.reshape(regions, CAP, vectors, padded), 'do...]
    all_to_all x1 -> x0, starting transfers between devices: 8.34 us -> none  [shards(): lax.all_to_all(product_buffer.reshape(regions, CAP, vectors, padded), 'do...]
    ppermute x0 -> x15, waiting for transfers between devices: none -> 7.32 us  [swapped_with_each(): part = lax.ppermute(part, axis, [(d, d ^ mask) for d in range(ways)])]
    dot_general x1, matrix products: 2.22 us -> 6.06 us  [shards(): jnp.einsum('ebc,ecm->ebm', block_inverse, interface_basis, preferred_elem...]
    unnamed x21 -> x23, local copies, waits for them, and re-layouts: 6.64 us -> 3.64 us
    dynamic_update_slice x0 -> x16, local copies, waits for them, and re-layouts: none -> 1.24 us  [swapped_with_each(): lax.dynamic_update_slice_in_dim(full, part, (here ^ mask) * height, axis=...]
    gather x1, local copies, waits for them, and re-layouts: 1.85 us -> 0.78 us  [shards(): product_buffer = extended[slot_tile]]
  transfers between devices with their start and end apart: 4 -> 18, of which waited for: 3 -> 4; matrix products, arithmetic and copies ran while one was open for 17% -> 16% of each run, Pallas kernels for 0% -> 0%
where the time goes in v1:
time: 90.4 us; the launch traced here: 90.2 us
  starting transfers between devices  37.6 us (42%)
  local copies, waits for them, and re-layouts  20.1 us (22%)
  matrix products  19.8 us (22%)
  waiting for transfers between devices  10.3 us (11%)
  other arithmetic  1.84 us (2%)
    ppermute x15, starting transfers between devices, swapped_with_each(): part = lax.ppermute(part, axis, [(d, d ^ mask) for d in range(ways)])  33.3 us
    slice x1, local copies, waits for them, and re-layouts, shards(): coupling[:middle]  11.4 us
    ppermute x15, waiting for transfers between devices, swapped_with_each(): part = lax.ppermute(part, axis, [(d, d ^ mask) for d in range(ways)])  7.32 us
    dot_general x1, matrix products, shards(): jnp.einsum('ebc,ecm->ebm', block_inverse, interface_basis, preferred_elem...  6.06 us
    ppermute x3, starting transfers between devices, group_sum(): value = value + lax.ppermute(value, axis, pairs)  4.3 us
    dot_general x1, matrix products, shards(): jnp.einsum('tkb,tbc->tkc', sources[:middle], coupling[:middle], preferred...  4.26 us
    unnamed x23, local copies, waits for them, and re-layouts  3.64 us
    ppermute x3, waiting for transfers between devices, group_sum(): value = value + lax.ppermute(value, axis, pairs)  2.96 us
  transfers between devices with their start and end apart: 18, of which 4 were waited for; matrix products, arithmetic and copies ran while one was open for 16% of the time, Pallas kernels for 0%

profile of v1, /device:TPU:0, one launch (start us, length us, event | category | flops | bytes accessed | tf_op | source)
XLA Modules:
  0.0 90.2 jit_solution(8882299802838040129)
XLA Ops:
  0.0 0.8 pad_add_fusion
  0.8 0.2 convert_reduce_fusion.1
  1.0 0.1 multiply_add_fusion
  1.1 0.1 fusion.32
  1.2 0.1 select_reduce_fusion
  1.3 11.4 %fusion.40 = (bf16[8,625,625]{2,0,1:T(8,128)(2,1)}, bf16[8,625,625]{2,0,1:T(8,128)(2,1)}) fusion(bf16[16,625,625]{2,0,1:T(8,128)(2,1)} %param.10), kind=kLoop, calls=%fused_computation.88 | loop fusion | bytes 25000000 | tf_op jit(solution)/shard_map/slice | solution.py:78
  12.7 2.3 %convolution_convert_fusion.1 = bf16[8,32,625]{2,1,0:T(8,128)(2,1)S(1)} fusion(bf16[8,32,625]{2,1,0:T(8,128)(2,1)S(1)} %copy-done.5, bf16[8,625,625]{2,0,1:T(8,128)(2,1)S(1)} %copy-done.2), kind=kOutput, calls=%fused_computation.22 | convolution fusion | flops 200160000 | bytes 6890000 | tf_op jit(solution)/shard_map/ekb,ebc->ekc/dot_general | solution.py:55
  15.0 1.5 %gather_fusion = bf16[16,32,625]{2,1,0:T(8,128)(2,1)} fusion(bf16[8,32,625]{2,1,0:T(8,128)(2,1)S(1)} %convolution_convert_fusion.1, s32[1024]{0:T(1024)S(1)} %pad_clamp_fusion.1), kind=kCustom, calls=%fused_computation | custom fusion | bytes 1280064 | tf_op jit(solution)/shard_map/gather | solution.py:71
  16.5 4.3 %fusion.19 = bf16[8,32,625]{2,1,0:T(8,128)(2,1)S(1)} fusion(bf16[16,32,625]{2,1,0:T(8,128)(2,1)} %gather_fusion, bf16[8,625,625]{2,0,1:T(8,128)(2,1)} %get-tuple-element.5), kind=kOutput, calls=%fused_computation.20 | convolution fusion | flops 200160000 | bytes 7210000 | tf_op jit(solution)/shard_map/tkb,tbc->tkc/dot_general | solution.py:75
  20.7 0.1 slice-done.3
  20.8 1.2 %fusion.22 = bf16[8,32,625]{2,1,0:T(8,128)(2,1)S(1)} fusion(bf16[16,32,625]{2,1,0:T(8,128)(2,1)S(1)} %copy-done.3, bf16[8,625,625]{2,0,1:T(8,128)(2,1)S(1)} %bitcast.33), kind=kOutput, calls=%fused_computation.21 | convolution fusion | flops 200160000 | bytes 7210000 | tf_op jit(solution)/shard_map/tkb,tbc->tkc/dot_general | solution.py:81
  22.2 0.1 pad_maximum_fusion.1
  22.3 0.1 and_select_fusion
  22.4 0.1 pad_maximum_fusion
  22.5 0.8 gather_fusion.1
  23.3 0.2 constant_dynamic-slice_fusion
  23.6 1.8 %collective-permute-start = (bf16[1,2,32,640]{3,2,1,0:T(8,128)(2,1)S(1)}, bf16[1,2,32,640]{3,2,1,0:T(8,128)(2,1)S(1)}, u32[]{:S(2)}, u32[]{:S(2)}) collective-permute-start(bf16[1,2,32,640]{3,2,1,0:T(8,128)(2,1)S(1)} %get-tuple-element.21), channel_id=1, source_target_pairs={{0,8},{8,0},{16,24},{24,16},{32,40},{40,32},{48,56},{56,48},{64,72... | collective-permute-start | bytes 245768 | tf_op jit(solution)/shard_map/ppermute | solution.py:21
  25.3 2.9 %collective-permute-start.1 = (bf16[1,2,32,640]{3,2,1,0:T(8,128)(2,1)S(1)}, bf16[1,2,32,640]{3,2,1,0:T(8,128)(2,1)S(1)}, u32[]{:S(2)}, u32[]{:S(2)}) collective-permute-start(bf16[1,2,32,640]{3,2,1,0:T(8,128)(2,1)S(1)} %get-tuple-element.20), channel_id=1, source_target_pairs={{0,16},{8,24},{16,0},{24,8},{32,48},{40,56},{48,32},{56,40},{64,80... | collective-permute-start | bytes 245768 | tf_op jit(solution)/shard_map/ppermute | solution.py:21
  28.2 0.1 collective-permute-start.2
  28.3 2.0 %collective-permute-start.3 = (bf16[1,2,32,640]{3,2,1,0:T(8,128)(2,1)S(1)}, bf16[1,2,32,640]{3,2,1,0:T(8,128)(2,1)S(1)}, u32[]{:S(2)}, u32[]{:S(2)}) collective-permute-start(bf16[1,2,32,640]{3,2,1,0:T(8,128)(2,1)S(1)} %get-tuple-element.18), channel_id=1, source_target_pairs={{0,32},{8,40},{16,48},{24,56},{32,0},{40,8},{48,16},{56,24},{64,96... | collective-permute-start | bytes 245768 | tf_op jit(solution)/shard_map/ppermute | solution.py:21
  30.4 6.1 %convolution_convert_fusion = bf16[8,625,64]{1,2,0:T(8,128)(2,1)} fusion(bf16[8,625,64]{1,2,0:T(8,128)(2,1)S(1)} %copy-done, bf16[8,625,625]{2,0,1:T(8,128)(2,1)} %param.9), kind=kOutput, calls=%fused_computation.13 | convolution fusion | flops 400320000 | bytes 7530000 | tf_op jit(solution)/shard_map/ebc,ecm->ebm/dot_general | solution.py:107
  36.4 0.7 broadcast_in_dim.46
  37.1 0.1 copy_dynamic-update-slice_fusion.15
  37.2 3.5 %copy.60 = bf16[8,625,625]{2,1,0:T(8,128)(2,1)} copy(bf16[8,625,625]{2,0,1:T(8,128)(2,1)S(1)} %bitcast.31) | data formatting | bytes 12500000 | tf_op args[1]
  40.8 5.2 %collective-permute-start.5 = (bf16[1,2,32,640]{3,2,1,0:T(8,128)(2,1)S(1)}, bf16[1,2,32,640]{3,2,1,0:T(8,128)(2,1)S(1)}, u32[]{:S(2)}, u32[]{:S(2)}) collective-permute-start(bf16[1,2,32,640]{3,2,1,0:T(8,128)(2,1)S(1)} %get-tuple-element.16), channel_id=1, source_target_pairs={{0,48},{8,56},{16,32},{24,40},{32,16},{40,24},{48,0},{56,8},{64,11... | collective-permute-start | bytes 245768 | tf_op jit(solution)/shard_map/ppermute | solution.py:21
  45.9 0.1 copy_dynamic-update-slice_fusion.14
  46.0 0.3 collective-permute-start.6
  46.3 0.1 copy_dynamic-update-slice_fusion.13
  46.4 3.9 %collective-permute-start.7 = (bf16[1,2,32,640]{3,2,1,0:T(8,128)(2,1)S(1)}, bf16[1,2,32,640]{3,2,1,0:T(8,128)(2,1)S(1)}, u32[]{:S(2)}, u32[]{:S(2)}) collective-permute-start(bf16[1,2,32,640]{3,2,1,0:T(8,128)(2,1)S(1)} %get-tuple-element.14), channel_id=1, source_target_pairs={{0,64},{8,72},{16,80},{24,88},{32,96},{40,104},{48,112},{56,120},{... | collective-permute-start | bytes 245768 | tf_op jit(solution)/shard_map/ppermute | solution.py:21
  50.3 0.1 copy_dynamic-update-slice_fusion.12
  50.4 0.3 collective-permute-start.8
  50.7 0.1 copy_dynamic-update-slice_fusion.11
  50.8 6.5 %collective-permute-start.9 = (bf16[1,2,32,640]{3,2,1,0:T(8,128)(2,1)S(1)}, bf16[1,2,32,640]{3,2,1,0:T(8,128)(2,1)S(1)}, u32[]{:S(2)}, u32[]{:S(2)}) collective-permute-start(bf16[1,2,32,640]{3,2,1,0:T(8,128)(2,1)S(1)} %get-tuple-element.12), channel_id=1, source_target_pairs={{0,80},{8,88},{16,64},{24,72},{32,112},{40,120},{48,96},{56,104},{... | collective-permute-start | bytes 245768 | tf_op jit(solution)/shard_map/ppermute | solution.py:21
  57.3 0.1 copy_dynamic-update-slice_fusion.10
  57.4 0.2 collective-permute-start.10
  57.6 0.1 copy_dynamic-update-slice_fusion.9
  57.7 3.4 %collective-permute-start.11 = (bf16[1,2,32,640]{3,2,1,0:T(8,128)(2,1)S(1)}, bf16[1,2,32,640]{3,2,1,0:T(8,128)(2,1)S(1)}, u32[]{:S(2)}, u32[]{:S(2)}) collective-permute-start(bf16[1,2,32,640]{3,2,1,0:T(8,128)(2,1)S(1)} %get-tuple-element.10), channel_id=1, source_target_pairs={{0,96},{8,104},{16,112},{24,120},{32,64},{40,72},{48,80},{56,88},{... | collective-permute-start | bytes 245768 | tf_op jit(solution)/shard_map/ppermute | solution.py:21
  61.0 0.1 copy_dynamic-update-slice_fusion.8
  61.1 0.1 collective-permute-start.12
  61.2 0.1 copy_dynamic-update-slice_fusion.7
  61.3 6.6 %collective-permute-start.13 = (bf16[1,2,32,640]{3,2,1,0:T(8,128)(2,1)S(1)}, bf16[1,2,32,640]{3,2,1,0:T(8,128)(2,1)S(1)}, u32[]{:S(2)}, u32[]{:S(2)}) collective-permute-start(bf16[1,2,32,640]{3,2,1,0:T(8,128)(2,1)S(1)} %get-tuple-element.8), channel_id=1, source_target_pairs={{0,112},{8,120},{16,96},{24,104},{32,80},{40,88},{48,64},{56,72},{... | collective-permute-start | bytes 245768 | tf_op jit(solution)/shard_map/ppermute | solution.py:21
  67.9 0.1 copy_dynamic-update-slice_fusion.6
  68.0 0.1 collective-permute-start.14
  68.1 0.1 copy_dynamic-update-slice_fusion.5
  68.2 0.1 copy_dynamic-update-slice_fusion.4
  68.3 0.1 copy_dynamic-update-slice_fusion.3
  68.4 0.1 copy_dynamic-update-slice_fusion.2
  68.5 2.7 %collective-permute-done.13 = bf16[1,2,32,640]{3,2,1,0:T(8,128)(2,1)S(1)} collective-permute-done((bf16[1,2,32,640]{3,2,1,0:T(8,128)(2,1)S(1)}, bf16[1,2,32,640]{3,2,1,0:T(8,128)(2,1)S(1)}, u32[]{:S(2)}, u32[]{:S(2)}) %collective-permute-start.13) | collective-permute-done | bytes 81952 | tf_op jit(solution)/shard_map/ppermute | solution.py:21
  71.2 0.1 copy_dynamic-update-slice_fusion.1
  71.2 4.6 %collective-permute-done.14 = bf16[1,2,32,640]{3,2,1,0:T(8,128)(2,1)S(1)} collective-permute-done((bf16[1,2,32,640]{3,2,1,0:T(8,128)(2,1)S(1)}, bf16[1,2,32,640]{3,2,1,0:T(8,128)(2,1)S(1)}, u32[]{:S(2)}, u32[]{:S(2)}) %collective-permute-start.14) | collective-permute-done | bytes 81952 | tf_op jit(solution)/shard_map/ppermute | solution.py:21
  75.9 0.1 copy_dynamic-update-slice_fusion
  75.9 0.5 reshape.53
  76.5 0.2 convert_reduce_fusion
  76.7 1.4 %fusion.16 = bf16[8,32,625]{2,0,1:T(8,128)(2,1)S(1)} fusion(bf16[32,32,640]{2,0,1:T(8,128)(2,1)S(1)} %reshape.53, bf16[8,32,625]{2,1,0:T(8,128)(2,1)} %param.8, s32[32]{0:T(128)S(1)} %convert_reduce_fusion), kind=kOutput, calls=%fused_computation.19 | convolution fusion | flops 10720256 | bytes 1950848 | tf_op jit(solution)/shard_map/es,skc->ekc/dot_general | solution.py:105
  78.1 0.3 convolution_bitcast_fusion.1
  78.4 0.1 fusion.41
  78.5 1.1 %collective-permute-done.15 = f32[32,64]{1,0:T(8,128)S(1)} collective-permute-done((f32[32,64]{1,0:T(8,128)S(1)}, f32[32,64]{1,0:T(8,128)S(1)}, u32[]{:S(2)}, u32[]{:S(2)}) %collective-permute-start.15) | collective-permute-done | bytes 8224 | tf_op jit(solution)/shard_map/ppermute | solution.py:33
  79.6 1.5 %collective-permute-start.16 = (f32[32,64]{1,0:T(8,128)S(1)}, f32[32,64]{1,0:T(8,128)S(1)}, u32[]{:S(2)}, u32[]{:S(2)}) collective-permute-start(f32[32,64]{1,0:T(8,128)S(1)} %add.117), channel_id=1, source_target_pairs={{0,2},{1,3},{2,0},{3,1},{4,6},{5,7},{6,4},{7,5},{8,10},{9,11},{10,... | collective-permute-start | bytes 24584 | tf_op jit(solution)/shard_map/ppermute | solution.py:33
  81.1 2.5 %fusion.4 = f32[4,32,625]{2,1,0:T(8,128)S(1)} fusion(bf16[8,625,625]{2,1,0:T(8,128)(2,1)} %copy.60, bf16[4,32,625]{2,0,1:T(4,128)(2,1)S(1)} %get-tuple-element.24), kind=kOutput, calls=%fused_computation.6 | convolution fusion | flops 100000000 | bytes 3715840 | tf_op jit(solution)/shard_map/ekb,ebc->ekc/dot_general | solution.py:126
  83.7 2.8 %collective-permute-start.17 = (f32[32,64]{1,0:T(8,128)S(1)}, f32[32,64]{1,0:T(8,128)S(1)}, u32[]{:S(2)}, u32[]{:S(2)}) collective-permute-start(f32[32,64]{1,0:T(8,128)S(1)} %add.118), channel_id=1, source_target_pairs={{0,4},{1,5},{2,6},{3,7},{4,0},{5,1},{6,2},{7,3},{8,12},{9,13},{10,... | collective-permute-start | bytes 24584 | tf_op jit(solution)/shard_map/ppermute | solution.py:33
  86.5 0.6 fusion.6
  87.1 1.9 %collective-permute-done.17 = f32[32,64]{1,0:T(8,128)S(1)} collective-permute-done((f32[32,64]{1,0:T(8,128)S(1)}, f32[32,64]{1,0:T(8,128)S(1)}, u32[]{:S(2)}, u32[]{:S(2)}) %collective-permute-start.17) | collective-permute-done | bytes 8224 | tf_op jit(solution)/shard_map/ppermute | solution.py:33
  89.0 0.1 fusion.25
  89.1 1.1 %fusion.15 = f32[8,32,625]{2,1,0:T(8,128)} fusion(bf16[32,64,1]{1,0,2:T(8,128)(2,1)S(1)} %fusion.25, bf16[8,625,64]{1,2,0:T(8,128)(2,1)S(1)} %copy-done, f32[4,32,625]{2,1,0:T(8,128)S(1)} %fusion.4, f32[4,32,625]{2,1,0:T(8,128)S(1)} %fusion.6), kind=kOutput, calls=%fused_computation.18 | convolution fusion | flops 20800000 | bytes 1924096 | tf_op jit(solution)/shard_map/km,ebm->ekb/dot_general | solution.py:141
  (49 shorter events, 0.3 us)
Async XLA Ops:
  0.0 30.4 %copy-start = (bf16[8,625,64]{1,2,0:T(8,128)(2,1)S(1)}, bf16[8,625,64]{1,2,0:T(8,128)(2,1)}, u32[]{:S(2)}) copy-start(bf16[8,625,64]{1,2,0:T(8,128)(2,1)} %param.14) | copy-start | bytes 1920004
  1.3 11.4 %copy-start.2 = (bf16[8,625,625]{2,0,1:T(8,128)(2,1)S(1)}, bf16[8,625,625]{2,0,1:T(8,128)(2,1)}, u32[]{:S(2)}) copy-start(bf16[8,625,625]{2,0,1:T(8,128)(2,1)} %param.9) | copy-start | bytes 18750004
  1.3 11.4 %copy-start.5 = (bf16[8,32,625]{2,1,0:T(8,128)(2,1)S(1)}, bf16[8,32,625]{2,1,0:T(8,128)(2,1)}, u32[]{:S(2)}) copy-start(bf16[8,32,625]{2,1,0:T(8,128)(2,1)} %param.8) | copy-start | bytes 960004
  15.0 5.7 %slice-start.2 = ((s8[6400000]{0:T(1024)(128)(4,1)}), s8[2205696]{0:T(1024)(128)(4,1)S(1)}, s32[]{:S(2)}) async-start(s8[6400000]{0:T(1024)(128)(4,1)} %bitcast.32), calls=%async_computation.2 | async-start | bytes 4411392
  16.5 4.4 %slice-start.3 = ((s8[6400000]{0:T(1024)(128)(4,1)}), s8[4194304]{0:T(1024)(128)(4,1)S(1)}, s32[]{:S(2)}) async-start(s8[6400000]{0:T(1024)(128)(4,1)} %bitcast.32), calls=%async_computation.3 | async-start | bytes 8388608
  16.5 4.4 %copy-start.3 = (bf16[16,32,625]{2,1,0:T(8,128)(2,1)S(1)}, bf16[16,32,625]{2,1,0:T(8,128)(2,1)}, u32[]{:S(2)}) copy-start(bf16[16,32,625]{2,1,0:T(8,128)(2,1)} %gather_fusion) | copy-start | bytes 1920004
  23.6 17.2 %collective-permute-start = (bf16[1,2,32,640]{3,2,1,0:T(8,128)(2,1)S(1)}, bf16[1,2,32,640]{3,2,1,0:T(8,128)(2,1)S(1)}, u32[]{:S(2)}, u32[]{:S(2)}) collective-permute-start(bf16[1,2,32,640]{3,2,1,0:T(8,128)(2,1)S(1)} %get-tuple-element.21), channel_id=1, source_target_pairs={{0,8},{8,0},{16,24},{24,16},{32,40},{40,32},{48,56},{56,48},{64,72... | collective-permute-start | bytes 245768 | tf_op jit(solution)/shard_map/ppermute | solution.py:21
  25.3 20.7 %collective-permute-start.1 = (bf16[1,2,32,640]{3,2,1,0:T(8,128)(2,1)S(1)}, bf16[1,2,32,640]{3,2,1,0:T(8,128)(2,1)S(1)}, u32[]{:S(2)}, u32[]{:S(2)}) collective-permute-start(bf16[1,2,32,640]{3,2,1,0:T(8,128)(2,1)S(1)} %get-tuple-element.20), channel_id=1, source_target_pairs={{0,16},{8,24},{16,0},{24,8},{32,48},{40,56},{48,32},{56,40},{64,80... | collective-permute-start | bytes 245768 | tf_op jit(solution)/shard_map/ppermute | solution.py:21
  28.2 18.2 %collective-permute-start.2 = (bf16[1,2,32,640]{3,2,1,0:T(8,128)(2,1)S(1)}, bf16[1,2,32,640]{3,2,1,0:T(8,128)(2,1)S(1)}, u32[]{:S(2)}, u32[]{:S(2)}) collective-permute-start(bf16[1,2,32,640]{3,2,1,0:T(8,128)(2,1)S(1)} %get-tuple-element.19), channel_id=1, source_target_pairs={{0,24},{8,16},{16,8},{24,0},{32,56},{40,48},{48,40},{56,32},{64,88... | collective-permute-start | bytes 245768 | tf_op jit(solution)/shard_map/ppermute | solution.py:21
  28.3 22.1 %collective-permute-start.3 = (bf16[1,2,32,640]{3,2,1,0:T(8,128)(2,1)S(1)}, bf16[1,2,32,640]{3,2,1,0:T(8,128)(2,1)S(1)}, u32[]{:S(2)}, u32[]{:S(2)}) collective-permute-start(bf16[1,2,32,640]{3,2,1,0:T(8,128)(2,1)S(1)} %get-tuple-element.18), channel_id=1, source_target_pairs={{0,32},{8,40},{16,48},{24,56},{32,0},{40,8},{48,16},{56,24},{64,96... | collective-permute-start | bytes 245768 | tf_op jit(solution)/shard_map/ppermute | solution.py:21
  30.4 6.8 %slice-start = ((s8[6400000]{0:T(1024)(128)(4,1)}), s8[4194304]{0:T(1024)(128)(4,1)S(1)}, s32[]{:S(2)}) async-start(s8[6400000]{0:T(1024)(128)(4,1)} %bitcast.30), calls=%async_computation | async-start | bytes 8388608
  30.4 6.8 %slice-start.1 = ((s8[6400000]{0:T(1024)(128)(4,1)}), s8[2205696]{0:T(1024)(128)(4,1)S(1)}, s32[]{:S(2)}) async-start(s8[6400000]{0:T(1024)(128)(4,1)} %bitcast.30), calls=%async_computation.1 | async-start | bytes 4411392
  30.4 20.4 %collective-permute-start.4 = (bf16[1,2,32,640]{3,2,1,0:T(8,128)(2,1)S(1)}, bf16[1,2,32,640]{3,2,1,0:T(8,128)(2,1)S(1)}, u32[]{:S(2)}, u32[]{:S(2)}) collective-permute-start(bf16[1,2,32,640]{3,2,1,0:T(8,128)(2,1)S(1)} %get-tuple-element.17), channel_id=1, source_target_pairs={{0,40},{8,32},{16,56},{24,48},{32,8},{40,0},{48,24},{56,16},{64,10... | collective-permute-start | bytes 245768 | tf_op jit(solution)/shard_map/ppermute | solution.py:21
  40.8 16.6 %collective-permute-start.5 = (bf16[1,2,32,640]{3,2,1,0:T(8,128)(2,1)S(1)}, bf16[1,2,32,640]{3,2,1,0:T(8,128)(2,1)S(1)}, u32[]{:S(2)}, u32[]{:S(2)}) collective-permute-start(bf16[1,2,32,640]{3,2,1,0:T(8,128)(2,1)S(1)} %get-tuple-element.16), channel_id=1, source_target_pairs={{0,48},{8,56},{16,32},{24,40},{32,16},{40,24},{48,0},{56,8},{64,11... | collective-permute-start | bytes 245768 | tf_op jit(solution)/shard_map/ppermute | solution.py:21
  46.0 11.6 %collective-permute-start.6 = (bf16[1,2,32,640]{3,2,1,0:T(8,128)(2,1)S(1)}, bf16[1,2,32,640]{3,2,1,0:T(8,128)(2,1)S(1)}, u32[]{:S(2)}, u32[]{:S(2)}) collective-permute-start(bf16[1,2,32,640]{3,2,1,0:T(8,128)(2,1)S(1)} %get-tuple-element.15), channel_id=1, source_target_pairs={{0,56},{8,48},{16,40},{24,32},{32,24},{40,16},{48,8},{56,0},{64,12... | collective-permute-start | bytes 245768 | tf_op jit(solution)/shard_map/ppermute | solution.py:21
  46.4 14.7 %collective-permute-start.7 = (bf16[1,2,32,640]{3,2,1,0:T(8,128)(2,1)S(1)}, bf16[1,2,32,640]{3,2,1,0:T(8,128)(2,1)S(1)}, u32[]{:S(2)}, u32[]{:S(2)}) collective-permute-start(bf16[1,2,32,640]{3,2,1,0:T(8,128)(2,1)S(1)} %get-tuple-element.14), channel_id=1, source_target_pairs={{0,64},{8,72},{16,80},{24,88},{32,96},{40,104},{48,112},{56,120},{... | collective-permute-start | bytes 245768 | tf_op jit(solution)/shard_map/ppermute | solution.py:21
  50.4 10.9 %collective-permute-start.8 = (bf16[1,2,32,640]{3,2,1,0:T(8,128)(2,1)S(1)}, bf16[1,2,32,640]{3,2,1,0:T(8,128)(2,1)S(1)}, u32[]{:S(2)}, u32[]{:S(2)}) collective-permute-start(bf16[1,2,32,640]{3,2,1,0:T(8,128)(2,1)S(1)} %get-tuple-element.13), channel_id=1, source_target_pairs={{0,72},{8,64},{16,88},{24,80},{32,104},{40,96},{48,120},{56,112},{... | collective-permute-start | bytes 245768 | tf_op jit(solution)/shard_map/ppermute | solution.py:21
  50.8 17.2 %collective-permute-start.9 = (bf16[1,2,32,640]{3,2,1,0:T(8,128)(2,1)S(1)}, bf16[1,2,32,640]{3,2,1,0:T(8,128)(2,1)S(1)}, u32[]{:S(2)}, u32[]{:S(2)}) collective-permute-start(bf16[1,2,32,640]{3,2,1,0:T(8,128)(2,1)S(1)} %get-tuple-element.12), channel_id=1, source_target_pairs={{0,80},{8,88},{16,64},{24,72},{32,112},{40,120},{48,96},{56,104},{... | collective-permute-start | bytes 245768 | tf_op jit(solution)/shard_map/ppermute | solution.py:21
  57.4 10.8 %collective-permute-start.10 = (bf16[1,2,32,640]{3,2,1,0:T(8,128)(2,1)S(1)}, bf16[1,2,32,640]{3,2,1,0:T(8,128)(2,1)S(1)}, u32[]{:S(2)}, u32[]{:S(2)}) collective-permute-start(bf16[1,2,32,640]{3,2,1,0:T(8,128)(2,1)S(1)} %get-tuple-element.11), channel_id=1, source_target_pairs={{0,88},{8,80},{16,72},{24,64},{32,120},{40,112},{48,104},{56,96},{... | collective-permute-start | bytes 245768 | tf_op jit(solution)/shard_map/ppermute | solution.py:21
  57.7 10.7 %collective-permute-start.11 = (bf16[1,2,32,640]{3,2,1,0:T(8,128)(2,1)S(1)}, bf16[1,2,32,640]{3,2,1,0:T(8,128)(2,1)S(1)}, u32[]{:S(2)}, u32[]{:S(2)}) collective-permute-start(bf16[1,2,32,640]{3,2,1,0:T(8,128)(2,1)S(1)} %get-tuple-element.10), channel_id=1, source_target_pairs={{0,96},{8,104},{16,112},{24,120},{32,64},{40,72},{48,80},{56,88},{... | collective-permute-start | bytes 245768 | tf_op jit(solution)/shard_map/ppermute | solution.py:21
  61.1 7.3 %collective-permute-start.12 = (bf16[1,2,32,640]{3,2,1,0:T(8,128)(2,1)S(1)}, bf16[1,2,32,640]{3,2,1,0:T(8,128)(2,1)S(1)}, u32[]{:S(2)}, u32[]{:S(2)}) collective-permute-start(bf16[1,2,32,640]{3,2,1,0:T(8,128)(2,1)S(1)} %get-tuple-element.9), channel_id=1, source_target_pairs={{0,104},{8,96},{16,120},{24,112},{32,72},{40,64},{48,88},{56,80},{... | collective-permute-start | bytes 245768 | tf_op jit(solution)/shard_map/ppermute | solution.py:21
  61.3 9.9 %collective-permute-start.13 = (bf16[1,2,32,640]{3,2,1,0:T(8,128)(2,1)S(1)}, bf16[1,2,32,640]{3,2,1,0:T(8,128)(2,1)S(1)}, u32[]{:S(2)}, u32[]{:S(2)}) collective-permute-start(bf16[1,2,32,640]{3,2,1,0:T(8,128)(2,1)S(1)} %get-tuple-element.8), channel_id=1, source_target_pairs={{0,112},{8,120},{16,96},{24,104},{32,80},{40,88},{48,64},{56,72},{... | collective-permute-start | bytes 245768 | tf_op jit(solution)/shard_map/ppermute | solution.py:21
  68.0 7.8 %collective-permute-start.14 = (bf16[1,2,32,640]{3,2,1,0:T(8,128)(2,1)S(1)}, bf16[1,2,32,640]{3,2,1,0:T(8,128)(2,1)S(1)}, u32[]{:S(2)}, u32[]{:S(2)}) collective-permute-start(bf16[1,2,32,640]{3,2,1,0:T(8,128)(2,1)S(1)} %get-tuple-element.7), channel_id=1, source_target_pairs={{0,120},{8,112},{16,104},{24,96},{32,88},{40,80},{48,72},{56,64},{... | collective-permute-start | bytes 245768 | tf_op jit(solution)/shard_map/ppermute | solution.py:21
  76.5 1.6 %copy-start.4 = (bf16[8,625,64]{1,2,0:T(8,128)(2,1)S(1)}, bf16[8,625,64]{1,2,0:T(8,128)(2,1)}, u32[]{:S(2)}) copy-start(bf16[8,625,64]{1,2,0:T(8,128)(2,1)} %convolution_convert_fusion) | copy-start | bytes 1920004
  76.7 9.8 %copy-start.1 = (bf16[8,625,625]{2,1,0:T(8,128)(2,1)S(1)}, bf16[8,625,625]{2,1,0:T(8,128)(2,1)}, u32[]{:S(2)}) copy-start(bf16[8,625,625]{2,1,0:T(8,128)(2,1)} %copy.60) | copy-start | bytes 18750004
  78.4 1.2 %collective-permute-start.15 = (f32[32,64]{1,0:T(8,128)S(1)}, f32[32,64]{1,0:T(8,128)S(1)}, u32[]{:S(2)}, u32[]{:S(2)}) collective-permute-start(f32[32,64]{1,0:T(8,128)S(1)} %convolution_bitcast_fusion.1), channel_id=1, source_target_pairs={{0,1},{1,0},{2,3},{3,2},{4,5},{5,4},{6,7},{7,6},{8,9},{9,8},{10,11... | collective-permute-start | bytes 24584 | tf_op jit(solution)/shard_map/ppermute | solution.py:33
  79.6 4.0 %collective-permute-start.16 = (f32[32,64]{1,0:T(8,128)S(1)}, f32[32,64]{1,0:T(8,128)S(1)}, u32[]{:S(2)}, u32[]{:S(2)}) collective-permute-start(f32[32,64]{1,0:T(8,128)S(1)} %add.117), channel_id=1, source_target_pairs={{0,2},{1,3},{2,0},{3,1},{4,6},{5,7},{6,4},{7,5},{8,10},{9,11},{10,... | collective-permute-start | bytes 24584 | tf_op jit(solution)/shard_map/ppermute | solution.py:33
  83.7 5.3 %collective-permute-start.17 = (f32[32,64]{1,0:T(8,128)S(1)}, f32[32,64]{1,0:T(8,128)S(1)}, u32[]{:S(2)}, u32[]{:S(2)}) collective-permute-start(f32[32,64]{1,0:T(8,128)S(1)} %add.118), channel_id=1, source_target_pairs={{0,4},{1,5},{2,6},{3,7},{4,0},{5,1},{6,2},{7,3},{8,12},{9,13},{10,... | collective-permute-start | bytes 24584 | tf_op jit(solution)/shard_map/ppermute | solution.py:33
  86.5 2.5 %copy-start.6 = (f32[1,64,64]{2,1,0:T(8,128)S(1)}, f32[1,64,64]{2,1,0:T(8,128)}, u32[]{:S(2)}) copy-start(f32[1,64,64]{2,1,0:T(8,128)} %param.15) | copy-start | bytes 49156
